TPU v7x, 128 devices: a whole 4x4x4 slice. The times are simulated.
128 devices in a mesh: head: 4 (over z), page: 32 (over x, y, core).
Axes of the slice: x: 4, y: 4, z: 4, core: 2. Of those that a mesh axis runs over, the one named last changes fastest.
Arguments:
- hidden_in: bfloat16 [32, 1024, 1024], P('page', 'head'), may hold values from -6 to 6
- norm_gain: float32 [1024], replicated, may hold values from 0.1 to 1.9
- w_qkv: bfloat16 [1024, 3, 1024], P(None, None, 'head'), may hold values from -0.1875 to 0.1875
- w_out: bfloat16 [1024, 1024], P('head'), may hold values from -0.75 to 0.75
- cache_kv: bfloat16 [2, 64, 128, 1024], P(None, 'page', None, 'head'), may hold values from -110 to 110, as said below
- page_node: int32 [64], replicated, may hold values from 0 to 18, as said below
- page_fill: int32 [64], replicated, may hold values from 1 to 128
- node_parent: int32 [19], replicated, may hold values from 0 to 2, as said below
- tok_seg: int32 [32, 1024], P('page'), may hold values from 0 to 7, never falling along the last dimension, each value on 1 to 256 neighbouring positions
- req_leaf: int32 [32, 8], P('page'), may hold values from 3 to 18, as said below
Outputs:
- attn_out: bfloat16 [32, 1024, 1024], P('page', 'head')
Inputs may be any that keep to these rules, and one draw needn't show every extreme that they name: `cache_kv`: entries of the cache; keys and values. `page_node`: every node owns at least one page. `node_parent`: node 0 is the root and its own parent; nodes 1 to 2 have parent 0; the others have a parent among nodes 1 to 2, and each of those has a child. `req_leaf`: each request names a lowest-level node; every lowest-level node is named by some request.
All inputs are finite; a program needn't handle non-finite values.
Results may differ from a plain program's by a relative error of at most 0.018.
Values may be sent and summed in bfloat16 or wider, within the bound.
No kernel may reach another device: no remote copies, remote signals or barrier semaphores. Data moves between devices by JAX's collectives and lax.ppermute only.
A program may use at most 64 MiB of HBM per device.

v0:
```python
import math

import jax
import jax.numpy as jnp
from jax import lax
from jax.sharding import PartitionSpec as P

HD = 64


EPSILON = 1e-06
FLOOR_SCORE = -1e30


def lookup(indices, lookup_table):
    matches = indices[:, None] == jnp.arange(lookup_table.shape[0], dtype=jnp.int32)[None, :]
    return jnp.sum(jnp.where(matches, lookup_table[None, :], 0), axis=1)


def shards(
    hidden_in,
    norm_gain,
    w_qkv,
    w_out,
    cache_kv,
    page_node,
    page_fill,
    node_parent,
    tok_seg,
    req_leaf,
):
    widened = hidden_in[0].astype(jnp.float32)
    normed = (
        widened
        * lax.rsqrt(jnp.mean(widened * widened, axis=1, keepdims=True) + EPSILON)
        * norm_gain
    ).astype(jnp.bfloat16)
    model_width = widened.shape[1]
    group_width = w_qkv.shape[2]
    head_size = HD
    group_heads = group_width // head_size
    weight_flat = w_qkv.reshape(model_width, 3 * group_width)
    projected = jnp.dot(
        lax.all_gather(normed, "head", axis=0, tiled=True),
        weight_flat,
        preferred_element_type=jnp.float32,
    ).astype(jnp.bfloat16)
    queries_all = projected.shape[0]
    queries = projected[:, :group_width].reshape(queries_all, group_heads, head_size)
    key_new = projected[:, group_width : 2 * group_width].reshape(
        queries_all, group_heads, head_size
    )
    value_new = projected[:, 2 * group_width :].reshape(queries_all, group_heads, head_size)
    score_scale = head_size ** (-0.5)
    segment = tok_seg[0]
    leaf_node = lookup(segment, req_leaf[0])
    upper_node = lookup(leaf_node, node_parent)
    root_node = lookup(upper_node, node_parent)
    position = jnp.arange(queries_all, dtype=jnp.int32)
    block_rows = min(queries_all, 512)

    def suffix_block(first):
        query_rows = lax.dynamic_slice_in_dim(queries, first, block_rows, 0)
        segment_rows = lax.dynamic_slice_in_dim(segment, first, block_rows, 0)
        position_rows = first + jnp.arange(block_rows, dtype=jnp.int32)
        visible = (segment_rows[:, None] == segment[None, :]) & (
            position[None, :] <= position_rows[:, None]
        )
        scores = (
            jnp.einsum("qhd,khd->hqk", query_rows, key_new, preferred_element_type=jnp.float32)
            * score_scale
        )
        scores = jnp.where(visible[None], scores, FLOOR_SCORE)
        row_max = jnp.max(scores, axis=2)
        weights = jnp.where(visible[None], jnp.exp(scores - row_max[:, :, None]), 0.0)
        row_sum = jnp.sum(weights, axis=2)
        weighted = jnp.einsum(
            "hqk,khd->hqd",
            weights.astype(jnp.bfloat16),
            value_new,
            preferred_element_type=jnp.float32,
        )
        return (row_max, row_sum, weighted)

    block_starts = jnp.arange(0, queries_all, block_rows, dtype=jnp.int32)
    block_max, block_sum, block_weighted = lax.map(suffix_block, block_starts)
    initial = (
        jnp.transpose(block_max, (1, 0, 2)).reshape(group_heads, queries_all),
        jnp.transpose(block_sum, (1, 0, 2)).reshape(group_heads, queries_all),
        jnp.transpose(block_weighted, (1, 0, 2, 3)).reshape(group_heads, queries_all, head_size),
    )
    page_len = cache_kv.shape[2]
    page_slot = jnp.arange(page_len, dtype=jnp.int32)
    shard_piece = lax.all_gather(cache_kv, "page", axis=1, tiled=True)
    piece_pages = shard_piece.shape[1]
    group_pages = math.gcd(piece_pages, 4)
    step_count = piece_pages // group_pages
    block_keys = group_pages * page_len
    key_blocks = shard_piece[0].reshape(step_count, block_keys, group_heads, head_size)
    value_blocks = shard_piece[1].reshape(step_count, block_keys, group_heads, head_size)
    key_nodes = jnp.repeat(page_node, page_len).reshape(step_count, block_keys)
    key_valid = (page_slot[None, :] < page_fill[:, None]).reshape(step_count, block_keys)

    def one_step(partial_value, inputs):
        row_max, row_sum, weighted = partial_value
        key_block, value_block, node_block, valid_block = inputs
        visible = (
            (node_block[None, :] == leaf_node[:, None])
            | (node_block[None, :] == upper_node[:, None])
            | (node_block[None, :] == root_node[:, None])
        ) & valid_block[None, :]
        scores = (
            jnp.einsum("qhd,khd->hqk", queries, key_block, preferred_element_type=jnp.float32)
            * score_scale
        )
        scores = jnp.where(visible[None], scores, FLOOR_SCORE)
        new_max = jnp.maximum(row_max, jnp.max(scores, axis=2))
        rescale = jnp.exp(row_max - new_max)
        weights = jnp.where(visible[None], jnp.exp(scores - new_max[:, :, None]), 0.0)
        row_sum = row_sum * rescale + jnp.sum(weights, axis=2)
        weighted = weighted * rescale[:, :, None] + jnp.einsum(
            "hqk,khd->hqd",
            weights.astype(jnp.bfloat16),
            value_block,
            preferred_element_type=jnp.float32,
        )
        return ((new_max, row_sum, weighted), None)

    result_state, unused = lax.scan(
        one_step, initial, (key_blocks, value_blocks, key_nodes, key_valid)
    )
    final_max, final_sum, final_weighted = result_state
    attention = (final_weighted / final_sum[:, :, None]).astype(jnp.bfloat16)
    attention = jnp.transpose(attention, (1, 0, 2)).reshape(queries_all, group_width)
    result = lax.psum_scatter(
        jnp.dot(attention, w_out, preferred_element_type=jnp.float32).astype(jnp.bfloat16),
        "head",
        scatter_dimension=0,
        tiled=True,
    )
    return result[None]


def solution(mesh):
    placed = (
        P("page", "head", None),
        P(),
        P(None, None, "head"),
        P("head", None),
        P(None, "page", None, "head"),
        P(),
        P(),
        P(),
        P("page", None),
        P("page", None),
    )
    return jax.shard_map(
        shards, mesh=mesh, in_specs=placed, out_specs=P("page", "head", None), check_vma=False
    )
```

profile of v0, /device:TPU:1, one launch (start us, length us, event | category | flops | bytes accessed | tf_op | source)
XLA Modules:
  0.0 339.6 jit_solution(15440758614901769843)
XLA Ops:
  16.4 27.6 %all-gather.3.cloned.1.call-done = bf16[1024,1024]{1,0:T(8,128)(2,1)} async-done(((bf16[256,1024]{1,0:T(8,128)(2,1)}), bf16[1024,1024]{1,0:T(8,128)(2,1)}) %all-gather.3.cloned.1.call-update) | async-done | bytes 2097168 | tf_op jit(solution)/shard_map/all_gather | solution.py:44
  48.4 24.0 %while.30 = (s32[]{:T(128)}, f32[2,4,512]{2,1,0:T(4,128)S(1)}, f32[2,4,512]{2,1,0:T(4,128)S(1)}, f32[2,4,512,64]{2,3,1,0:T(8,128)S(1)}, s32[2]{0:T(128)S(1)}, /*...) while((s32[]{:T(128)}, f32[2,4,512]{2,1,0:T(4,128)S(1)}, ...), condition=%wide.region_4.5_spmd.clone, body=%wide.region_1.4_spmd.clone.sunk | while | flops 565703168 | bytes 29178048 | solution.py:86
  72.5 27.1 %all-gather.5.cloned.1.call-done = bf16[2,64,128,256]{3,2,1,0:T(8,128)(2,1)} async-done(((bf16[2,2,128,256]{3,2,1,0:T(8,128)(2,1)}), bf16[2,64,128,256]{3,2,1,0:T(8,128)(2,1)}) %all-gather.5.cloned.1.call-update) | async-done | bytes 8388624 | tf_op jit(solution)/shard_map/all_gather | solution.py:94
  99.5 6.0 %fusion.43 = (bf16[1,64,128,256]{3,2,1,0:T(8,128)(2,1)}, bf16[1,64,128,256]{3,2,1,0:T(8,128)(2,1)}) fusion(bf16[2,64,128,256]{3,2,1,0:T(8,128)(2,1)} %all-gather.5.cloned.1.call-done), kind=kLoop, calls=%fused_computation.63 | loop fusion | bytes 16777216 | tf_op jit(solution)/shard_map/slice | solution.py:100
  105.5 12.9 %reshape.224 = bf16[16,512,4,64]{3,2,1,0:T(4,128)(2,1)} reshape(bf16[1,64,128,256]{3,2,1,0:T(8,128)(2,1)} %get-tuple-element.231) | data formatting | bytes 8388608 | tf_op jit(solution)/shard_map/reshape;squeeze | solution.py:99
  118.4 12.7 %copy.24 = bf16[16,512,4,64]{1,3,2,0:T(8,128)(2,1)} copy(bf16[16,512,4,64]{3,2,1,0:T(4,128)(2,1)} %reshape.224) | data formatting | bytes 8388608 | tf_op jit(solution)/shard_map/while | solution.py:129
  131.1 12.9 %reshape.225 = bf16[16,512,4,64]{3,2,1,0:T(4,128)(2,1)} reshape(bf16[1,64,128,256]{3,2,1,0:T(8,128)(2,1)} %get-tuple-element.230) | data formatting | bytes 8388608 | tf_op jit(solution)/shard_map/reshape;squeeze | solution.py:100
  144.0 12.7 %copy.25 = bf16[16,512,4,64]{1,3,2,0:T(8,128)(2,1)} copy(bf16[16,512,4,64]{3,2,1,0:T(4,128)(2,1)} %reshape.225) | data formatting | bytes 8388608 | tf_op jit(solution)/shard_map/while | solution.py:129
  156.7 145.0 %while.29 = (s32[]{:T(128)}, f32[4,1024]{1,0:T(4,128)S(1)}, f32[4,1024]{1,0:T(4,128)S(1)}, f32[4,1024,64]{1,2,0:T(8,128)S(1)}, s32[16,512]{1,0:T(8,128)S(1)}, /*...) while((s32[]{:T(128)}, f32[4,1024]{1,0:T(4,128)S(1)}, ...), condition=%wide.region_11.12_spmd, body=%wide.region_8.11_spmd.sunk | while | flops 567812096 | bytes 30691972 | solution.py:129
  162.0 3.6 %fusion.70 = f32[4,1024,64]{1,2,0:T(8,128)S(1)} fusion(f32[4,512,1024]{2,1,0:T(8,128)S(1)} %get-tuple-element.368, f32[4,1024]{1,0:T(4,128)S(1)} %max.4, pred[1024,512]{0,1:T(8,128)(4,1)S(1)} %or_and_fusion.2, f32[4,1024,64]{1,2,0:T(8,128)S(1)} %get-tuple-element.440, f32[4,1024]{1,0:T(4,128)S(1)} %get-tuple-element.370, ...), kind=kOutput, calls=%fused_computation.29.clone.1 | convolution fusion | flops 279445504 | bytes 11305472 | tf_op jit(solution)/shard_map/while/body/eval_jaxpr/hqk,khd->hqd/dot_general | solution.py:121
  171.1 3.6 %fusion.70 = f32[4,1024,64]{1,2,0:T(8,128)S(1)} fusion(f32[4,512,1024]{2,1,0:T(8,128)S(1)} %get-tuple-element.368, f32[4,1024]{1,0:T(4,128)S(1)} %max.4, pred[1024,512]{0,1:T(8,128)(4,1)S(1)} %or_and_fusion.2, f32[4,1024,64]{1,2,0:T(8,128)S(1)} %get-tuple-element.440, f32[4,1024]{1,0:T(4,128)S(1)} %get-tuple-element.370, ...), kind=kOutput, calls=%fused_computation.29.clone.1 | convolution fusion | flops 279445504 | bytes 11305472 | tf_op jit(solution)/shard_map/while/body/eval_jaxpr/hqk,khd->hqd/dot_general | solution.py:121
  180.2 3.6 %fusion.70 = f32[4,1024,64]{1,2,0:T(8,128)S(1)} fusion(f32[4,512,1024]{2,1,0:T(8,128)S(1)} %get-tuple-element.368, f32[4,1024]{1,0:T(4,128)S(1)} %max.4, pred[1024,512]{0,1:T(8,128)(4,1)S(1)} %or_and_fusion.2, f32[4,1024,64]{1,2,0:T(8,128)S(1)} %get-tuple-element.440, f32[4,1024]{1,0:T(4,128)S(1)} %get-tuple-element.370, ...), kind=kOutput, calls=%fused_computation.29.clone.1 | convolution fusion | flops 279445504 | bytes 11305472 | tf_op jit(solution)/shard_map/while/body/eval_jaxpr/hqk,khd->hqd/dot_general | solution.py:121
  189.2 3.6 %fusion.70 = f32[4,1024,64]{1,2,0:T(8,128)S(1)} fusion(f32[4,512,1024]{2,1,0:T(8,128)S(1)} %get-tuple-element.368, f32[4,1024]{1,0:T(4,128)S(1)} %max.4, pred[1024,512]{0,1:T(8,128)(4,1)S(1)} %or_and_fusion.2, f32[4,1024,64]{1,2,0:T(8,128)S(1)} %get-tuple-element.440, f32[4,1024]{1,0:T(4,128)S(1)} %get-tuple-element.370, ...), kind=kOutput, calls=%fused_computation.29.clone.1 | convolution fusion | flops 279445504 | bytes 11305472 | tf_op jit(solution)/shard_map/while/body/eval_jaxpr/hqk,khd->hqd/dot_general | solution.py:121
  198.3 3.6 %fusion.70 = f32[4,1024,64]{1,2,0:T(8,128)S(1)} fusion(f32[4,512,1024]{2,1,0:T(8,128)S(1)} %get-tuple-element.368, f32[4,1024]{1,0:T(4,128)S(1)} %max.4, pred[1024,512]{0,1:T(8,128)(4,1)S(1)} %or_and_fusion.2, f32[4,1024,64]{1,2,0:T(8,128)S(1)} %get-tuple-element.440, f32[4,1024]{1,0:T(4,128)S(1)} %get-tuple-element.370, ...), kind=kOutput, calls=%fused_computation.29.clone.1 | convolution fusion | flops 279445504 | bytes 11305472 | tf_op jit(solution)/shard_map/while/body/eval_jaxpr/hqk,khd->hqd/dot_general | solution.py:121
  207.4 3.6 %fusion.70 = f32[4,1024,64]{1,2,0:T(8,128)S(1)} fusion(f32[4,512,1024]{2,1,0:T(8,128)S(1)} %get-tuple-element.368, f32[4,1024]{1,0:T(4,128)S(1)} %max.4, pred[1024,512]{0,1:T(8,128)(4,1)S(1)} %or_and_fusion.2, f32[4,1024,64]{1,2,0:T(8,128)S(1)} %get-tuple-element.440, f32[4,1024]{1,0:T(4,128)S(1)} %get-tuple-element.370, ...), kind=kOutput, calls=%fused_computation.29.clone.1 | convolution fusion | flops 279445504 | bytes 11305472 | tf_op jit(solution)/shard_map/while/body/eval_jaxpr/hqk,khd->hqd/dot_general | solution.py:121
  216.4 3.6 %fusion.70 = f32[4,1024,64]{1,2,0:T(8,128)S(1)} fusion(f32[4,512,1024]{2,1,0:T(8,128)S(1)} %get-tuple-element.368, f32[4,1024]{1,0:T(4,128)S(1)} %max.4, pred[1024,512]{0,1:T(8,128)(4,1)S(1)} %or_and_fusion.2, f32[4,1024,64]{1,2,0:T(8,128)S(1)} %get-tuple-element.440, f32[4,1024]{1,0:T(4,128)S(1)} %get-tuple-element.370, ...), kind=kOutput, calls=%fused_computation.29.clone.1 | convolution fusion | flops 279445504 | bytes 11305472 | tf_op jit(solution)/shard_map/while/body/eval_jaxpr/hqk,khd->hqd/dot_general | solution.py:121
  225.5 3.6 %fusion.70 = f32[4,1024,64]{1,2,0:T(8,128)S(1)} fusion(f32[4,512,1024]{2,1,0:T(8,128)S(1)} %get-tuple-element.368, f32[4,1024]{1,0:T(4,128)S(1)} %max.4, pred[1024,512]{0,1:T(8,128)(4,1)S(1)} %or_and_fusion.2, f32[4,1024,64]{1,2,0:T(8,128)S(1)} %get-tuple-element.440, f32[4,1024]{1,0:T(4,128)S(1)} %get-tuple-element.370, ...), kind=kOutput, calls=%fused_computation.29.clone.1 | convolution fusion | flops 279445504 | bytes 11305472 | tf_op jit(solution)/shard_map/while/body/eval_jaxpr/hqk,khd->hqd/dot_general | solution.py:121
  234.5 3.6 %fusion.70 = f32[4,1024,64]{1,2,0:T(8,128)S(1)} fusion(f32[4,512,1024]{2,1,0:T(8,128)S(1)} %get-tuple-element.368, f32[4,1024]{1,0:T(4,128)S(1)} %max.4, pred[1024,512]{0,1:T(8,128)(4,1)S(1)} %or_and_fusion.2, f32[4,1024,64]{1,2,0:T(8,128)S(1)} %get-tuple-element.440, f32[4,1024]{1,0:T(4,128)S(1)} %get-tuple-element.370, ...), kind=kOutput, calls=%fused_computation.29.clone.1 | convolution fusion | flops 279445504 | bytes 11305472 | tf_op jit(solution)/shard_map/while/body/eval_jaxpr/hqk,khd->hqd/dot_general | solution.py:121
  243.6 3.6 %fusion.70 = f32[4,1024,64]{1,2,0:T(8,128)S(1)} fusion(f32[4,512,1024]{2,1,0:T(8,128)S(1)} %get-tuple-element.368, f32[4,1024]{1,0:T(4,128)S(1)} %max.4, pred[1024,512]{0,1:T(8,128)(4,1)S(1)} %or_and_fusion.2, f32[4,1024,64]{1,2,0:T(8,128)S(1)} %get-tuple-element.440, f32[4,1024]{1,0:T(4,128)S(1)} %get-tuple-element.370, ...), kind=kOutput, calls=%fused_computation.29.clone.1 | convolution fusion | flops 279445504 | bytes 11305472 | tf_op jit(solution)/shard_map/while/body/eval_jaxpr/hqk,khd->hqd/dot_general | solution.py:121
  252.7 3.6 %fusion.70 = f32[4,1024,64]{1,2,0:T(8,128)S(1)} fusion(f32[4,512,1024]{2,1,0:T(8,128)S(1)} %get-tuple-element.368, f32[4,1024]{1,0:T(4,128)S(1)} %max.4, pred[1024,512]{0,1:T(8,128)(4,1)S(1)} %or_and_fusion.2, f32[4,1024,64]{1,2,0:T(8,128)S(1)} %get-tuple-element.440, f32[4,1024]{1,0:T(4,128)S(1)} %get-tuple-element.370, ...), kind=kOutput, calls=%fused_computation.29.clone.1 | convolution fusion | flops 279445504 | bytes 11305472 | tf_op jit(solution)/shard_map/while/body/eval_jaxpr/hqk,khd->hqd/dot_general | solution.py:121
  261.7 3.6 %fusion.70 = f32[4,1024,64]{1,2,0:T(8,128)S(1)} fusion(f32[4,512,1024]{2,1,0:T(8,128)S(1)} %get-tuple-element.368, f32[4,1024]{1,0:T(4,128)S(1)} %max.4, pred[1024,512]{0,1:T(8,128)(4,1)S(1)} %or_and_fusion.2, f32[4,1024,64]{1,2,0:T(8,128)S(1)} %get-tuple-element.440, f32[4,1024]{1,0:T(4,128)S(1)} %get-tuple-element.370, ...), kind=kOutput, calls=%fused_computation.29.clone.1 | convolution fusion | flops 279445504 | bytes 11305472 | tf_op jit(solution)/shard_map/while/body/eval_jaxpr/hqk,khd->hqd/dot_general | solution.py:121
  270.8 3.6 %fusion.70 = f32[4,1024,64]{1,2,0:T(8,128)S(1)} fusion(f32[4,512,1024]{2,1,0:T(8,128)S(1)} %get-tuple-element.368, f32[4,1024]{1,0:T(4,128)S(1)} %max.4, pred[1024,512]{0,1:T(8,128)(4,1)S(1)} %or_and_fusion.2, f32[4,1024,64]{1,2,0:T(8,128)S(1)} %get-tuple-element.440, f32[4,1024]{1,0:T(4,128)S(1)} %get-tuple-element.370, ...), kind=kOutput, calls=%fused_computation.29.clone.1 | convolution fusion | flops 279445504 | bytes 11305472 | tf_op jit(solution)/shard_map/while/body/eval_jaxpr/hqk,khd->hqd/dot_general | solution.py:121
  298.0 3.6 %fusion.70 = f32[4,1024,64]{1,2,0:T(8,128)S(1)} fusion(f32[4,512,1024]{2,1,0:T(8,128)S(1)} %get-tuple-element.368, f32[4,1024]{1,0:T(4,128)S(1)} %max.4, pred[1024,512]{0,1:T(8,128)(4,1)S(1)} %or_and_fusion.2, f32[4,1024,64]{1,2,0:T(8,128)S(1)} %get-tuple-element.440, f32[4,1024]{1,0:T(4,128)S(1)} %get-tuple-element.370, ...), kind=kOutput, calls=%fused_computation.29.clone.1 | convolution fusion | flops 279445504 | bytes 11305472 | tf_op jit(solution)/shard_map/while/body/eval_jaxpr/hqk,khd->hqd/dot_general | solution.py:121
  303.9 29.2 %reduce-scatter.2.cloned.1.call-done = bf16[256,1024]{1,0:T(8,128)(2,1)} async-done(((bf16[1024,1024]{1,0:T(8,128)(2,1)}), bf16[256,1024]{1,0:T(8,128)(2,1)}) %reduce-scatter.2.cloned.1.call-update) | async-done | bytes 524304 | tf_op jit(solution)/shard_map/reduce_scatter | solution.py:135
  (179 shorter events, 129.7 us)
Async XLA Ops:
  6.5 295.2 %copy-start = (bf16[256,1024]{1,0:T(8,128)(2,1)S(1)}, bf16[256,1024]{1,0:T(8,128)(2,1)}, u32[]{:S(2)}) copy-start(bf16[256,1024]{1,0:T(8,128)(2,1)} %param.17) | copy-start | bytes 1572868
  6.5 37.5 %all-gather.3.cloned.1.call-start = ((), (), s32[]{:S(2)}) async-start(), calls=%async_computation.1 | async-start | bytes 2621440 | tf_op jit(solution)/shard_map/all_gather | solution.py:44
  9.9 89.7 %all-gather.5.cloned.1.call-start = ((), (), s32[]{:S(2)}) async-start(), calls=%async_computation.2 | async-start | bytes 8650752 | tf_op jit(solution)/shard_map/all_gather | solution.py:94
  10.6 322.5 %reduce-scatter.2.cloned.1.call-start = ((), (), s32[]{:S(2)}) async-start(), calls=%async_computation.3 | async-start | bytes 2621440 | tf_op jit(solution)/shard_map/reduce_scatter | solution.py:135
  10.7 37.7 %copy-start.1 = (s32[1,1024]{1,0:T(1,128)S(1)}, s32[1,1024]{1,0:T(1,128)}, u32[]{:S(2)}) copy-start(s32[1,1024]{1,0:T(1,128)} %param.22) | copy-start | bytes 12292
Sparse Core Ops, SparseCore 0:
  10.0 34.0 all-gather.2
  46.4 53.0 all-gather.4
  304.0 29.0 reduce-scatter.1
where the time goes:
time: 342 us; the launch traced here: 340 us
  matrix products  116 us (34%)
  waiting for transfers between devices  84.7 us (25%)
  local copies, waits for them, and re-layouts  63.5 us (19%)
  other arithmetic  57.9 us (17%)
  between operations  13.2 us (4%)
  loops' own time  4.56 us (1%)
    dot_general x16, matrix products, one_step(): jnp.einsum('hqk,khd->hqd', weights.astype(jnp.bfloat16), value_block, pre...  58.4 us
    dot_general x16, matrix products, one_step(): jnp.einsum('qhd,khd->hqk', queries, key_block, preferred_element_type=jnp...  40.8 us
    reduce_sum x16, other arithmetic, one_step(): row_sum = row_sum * rescale + jnp.sum(weights, axis=2)  33.7 us
    reduce_scatter x1, waiting for transfers between devices, shards(): lax.psum_scatter(jnp.dot(attention, w_out, preferred_element_type=jnp.flo...  29.2 us
    all_gather x1, waiting for transfers between devices, shards(): lax.all_gather(normed, 'head', axis=0, tiled=True)  27.6 us
    all_gather x1, waiting for transfers between devices, shards(): shard_piece = lax.all_gather(cache_kv, 'page', axis=1, tiled=True)  27.1 us
    while x2, local copies, waits for them, and re-layouts, shards(): lax.scan(one_step, initial, (key_blocks, value_blocks, key_nodes, key_val...  25.4 us
    another operation x1, local copies, waits for them, and re-layouts, shards(): shard_piece[0].reshape(step_count, block_keys, group_heads, head_size)  12.9 us
  transfers between devices with their start and end apart: 3, of which 3 were waited for; matrix products, arithmetic and copies ran while one was open for 9% of the time, Pallas kernels for 0%

commit v1 on v0

v1 whole, which is shorter than its diff:
```python
import functools

import jax
import jax.numpy as jnp
from jax import lax
from jax.experimental import pallas as pl
from jax.experimental.pallas import tpu as pltpu
from jax.sharding import PartitionSpec as P

HD = 64
EPSILON = 1e-06
FLOOR_SCORE = -1e30
Q_BLOCK = 128
K_BLOCK = 128
INTERPRET = False


def lookup(indices, lookup_table):
    matches = indices[:, None] == jnp.arange(lookup_table.shape[0], dtype=jnp.int32)[None, :]
    return jnp.sum(jnp.where(matches, lookup_table[None, :], 0), axis=1)


def attn_kernel(
    vis_ref, pnode_ref, pfill_ref, kfirst_ref,
    q_ref, tok_ref, kn_ref, vn_ref, segk_ref, cache_ref,
    o_ref,
    m_sc, l_sc, acc_sc,
):
    i = pl.program_id(0)
    tq, width = q_ref.shape
    groups = width // HD
    pages = cache_ref.shape[1]
    kb = cache_ref.shape[2]
    q = q_ref[...] * jnp.asarray(0.125, jnp.bfloat16)
    seg_q = tok_ref[:, 0:1]
    leaf = tok_ref[:, 1:2]
    upper = tok_ref[:, 2:3]
    root = tok_ref[:, 3:4]
    m_sc[...] = jnp.full(m_sc.shape, FLOOR_SCORE, jnp.float32)
    l_sc[...] = jnp.zeros(l_sc.shape, jnp.float32)
    acc_sc[...] = jnp.zeros(acc_sc.shape, jnp.float32)
    col_head = lax.broadcasted_iota(jnp.int32, (kb, width), 1) // HD
    lane = lax.broadcasted_iota(jnp.int32, (1, kb), 1)
    half = lax.broadcasted_iota(jnp.int32, (1, 128), 1) < HD

    def block_diag(x):
        zero = jnp.zeros_like(x)
        return jnp.concatenate([jnp.where(col_head == h, x, zero) for h in range(groups)], axis=0)

    def update(k, v, mask):
        s = lax.dot_general(
            q, block_diag(k), (((1,), (1,)), ((), ())), preferred_element_type=jnp.float32
        )
        probs = []
        alphas = []
        for h in range(groups):
            s_h = jnp.where(mask, s[:, h * kb:(h + 1) * kb], FLOOR_SCORE)
            m_old = m_sc[h]
            m_new = jnp.maximum(m_old, jnp.max(s_h, axis=1, keepdims=True))
            alpha = jnp.exp(m_old - m_new)
            p_h = jnp.where(mask, jnp.exp(s_h - m_new), 0.0)
            l_sc[h] = alpha * l_sc[h] + jnp.sum(p_h, axis=1, keepdims=True)
            m_sc[h] = m_new
            probs.append(p_h.astype(jnp.bfloat16))
            alphas.append(alpha)
        pv = jnp.dot(
            jnp.concatenate(probs, axis=1), block_diag(v), preferred_element_type=jnp.float32
        )
        scale = jnp.concatenate(
            [
                jnp.where(half, alphas[2 * c], alphas[2 * c + 1])
                for c in range(groups // 2)
            ],
            axis=1,
        )
        acc_sc[...] = acc_sc[...] * scale + pv

    def page_step(g, carry):
        @pl.when(vis_ref[i * pages + g] > 0)
        def _():
            node = pnode_ref[g]
            fill = pfill_ref[g]
            tok_ok = (leaf == node) | (upper == node) | (root == node)
            mask = tok_ok & (lane < fill)
            update(cache_ref[0, g], cache_ref[1, g], mask)

        return carry

    lax.fori_loop(0, pages, page_step, 0)

    qpos = i * tq + lax.broadcasted_iota(jnp.int32, (tq, 1), 0)

    def suffix_step(b, carry):
        start = pl.multiple_of(b * kb, kb)
        kpos = start + lane
        mask = (seg_q == segk_ref[pl.ds(b, 1), :]) & (kpos <= qpos)
        update(kn_ref[pl.ds(start, kb), :], vn_ref[pl.ds(start, kb), :], mask)
        return carry

    last = (i * tq + tq - 1) // kb
    lax.fori_loop(kfirst_ref[i], last + 1, suffix_step, 0)

    norm = jnp.concatenate(
        [jnp.where(half, l_sc[2 * c], l_sc[2 * c + 1]) for c in range(groups // 2)], axis=1
    )
    o_ref[...] = (acc_sc[...] / norm).astype(o_ref.dtype)


def attention(vis, page_node, page_fill, kfirst, proj, tok, segk, cache):
    tokens = proj.shape[0]
    width = proj.shape[1] // 3
    groups = width // HD
    nqb = tokens // Q_BLOCK
    grid_spec = pltpu.PrefetchScalarGridSpec(
        num_scalar_prefetch=4,
        grid=(nqb,),
        in_specs=[
            pl.BlockSpec((Q_BLOCK, width), lambda i, *_: (i, 0)),
            pl.BlockSpec((Q_BLOCK, tok.shape[1]), lambda i, *_: (i, 0)),
            pl.BlockSpec((tokens, width), lambda i, *_: (0, 1)),
            pl.BlockSpec((tokens, width), lambda i, *_: (0, 2)),
            pl.BlockSpec(memory_space=pltpu.VMEM),
            pl.BlockSpec(memory_space=pltpu.VMEM),
        ],
        out_specs=pl.BlockSpec((Q_BLOCK, width), lambda i, *_: (i, 0)),
        scratch_shapes=[
            pltpu.VMEM((groups, Q_BLOCK, 1), jnp.float32),
            pltpu.VMEM((groups, Q_BLOCK, 1), jnp.float32),
            pltpu.VMEM((Q_BLOCK, width), jnp.float32),
        ],
    )
    return pl.pallas_call(
        attn_kernel,
        grid_spec=grid_spec,
        interpret=INTERPRET,
        out_shape=jax.ShapeDtypeStruct((tokens, width), jnp.bfloat16),
        compiler_params=pltpu.CompilerParams(
            dimension_semantics=("arbitrary",), vmem_limit_bytes=48 * 1024 * 1024
        ),
    )(vis, page_node, page_fill, kfirst, proj, tok, proj, proj, segk, cache)


def shards(
    hidden_in,
    norm_gain,
    w_qkv,
    w_out,
    cache_kv,
    page_node,
    page_fill,
    node_parent,
    tok_seg,
    req_leaf,
):
    widened = hidden_in[0].astype(jnp.float32)
    normed = (
        widened
        * lax.rsqrt(jnp.mean(widened * widened, axis=1, keepdims=True) + EPSILON)
        * norm_gain
    ).astype(jnp.bfloat16)
    model_width = widened.shape[1]
    group_width = w_qkv.shape[2]
    weight_flat = w_qkv.reshape(model_width, 3 * group_width)
    projected = jnp.dot(
        lax.all_gather(normed, "head", axis=0, tiled=True),
        weight_flat,
        preferred_element_type=jnp.float32,
    ).astype(jnp.bfloat16)
    tokens = projected.shape[0]
    segment = tok_seg[0]
    leaf_node = lookup(segment, req_leaf[0])
    upper_node = lookup(leaf_node, node_parent)
    root_node = lookup(upper_node, node_parent)
    tok = jnp.stack([segment, leaf_node, upper_node, root_node], axis=1)
    page_len = cache_kv.shape[2]
    pages = page_node.shape[0]
    seen = (
        (page_node[None, :] == leaf_node[:, None])
        | (page_node[None, :] == upper_node[:, None])
        | (page_node[None, :] == root_node[:, None])
    )
    nqb = tokens // Q_BLOCK
    vis = jnp.any(seen.reshape(nqb, Q_BLOCK, pages), axis=1).astype(jnp.int32).reshape(-1)
    first_seg = segment[::Q_BLOCK]
    kfirst = (
        jnp.sum((segment[None, :] < first_seg[:, None]).astype(jnp.int32), axis=1) // K_BLOCK
    ).astype(jnp.int32)
    segk = segment.reshape(tokens // K_BLOCK, K_BLOCK)
    cache = lax.all_gather(cache_kv, "page", axis=1, tiled=True)
    attn = attention(vis, page_node, page_fill, kfirst, projected, tok, segk, cache)
    result = lax.psum_scatter(
        jnp.dot(attn, w_out, preferred_element_type=jnp.float32).astype(jnp.bfloat16),
        "head",
        scatter_dimension=0,
        tiled=True,
    )
    return result[None]


def solution(mesh):
    placed = (
        P("page", "head", None),
        P(),
        P(None, None, "head"),
        P("head", None),
        P(None, "page", None, "head"),
        P(),
        P(),
        P(),
        P("page", None),
        P("page", None),
    )
    return jax.shard_map(
        shards, mesh=mesh, in_specs=placed, out_specs=P("page", "head", None), check_vma=False
    )
```

time: 342 us -> 237 us (0.69)
  matrix products: 116 us -> 5.95 us
  Pallas kernels: 0 us -> 92.4 us
  local copies, waits for them, and re-layouts: 63.5 us -> 2.14 us
  other arithmetic: 57.9 us -> 4.18 us
  waiting for transfers between devices: 84.7 us -> 117 us
  loops' own time: 4.56 us -> 0 us
    dot_general x37 -> x1, matrix products: 112 us -> 2.07 us  [shards(): jnp.dot(attn, w_out, preferred_element_type=jnp.float32)]
    pallas_call x0 -> x1, Pallas kernels: none -> 92.4 us  [attention(): pl.pallas_call(attn_kernel, grid_spec=grid_spec, interpret=INTERPRET, out...]
    reduce_sum x18 -> x1, other arithmetic: 39.6 us -> 0.19 us  [shards(): jnp.sum((segment[None, :] < first_seg[:, None]).astype(jnp.int32), axis=1)]
    another operation x2 -> x1, local copies, waits for them, and re-layouts: 25.8 us -> 0.22 us  [shards(): tok = jnp.stack([segment, leaf_node, upper_node, root_node], axis=1)]
    while x18 -> x0, local copies, waits for them, and re-layouts: 25.5 us -> none  [the longest x2 25.4 us: shards(): lax.scan(one_step, initial, (key_blocks, value_blocks, key_nodes, key_val...]
    all_gather x1, waiting for transfers between devices: 27.1 us -> 51.6 us  [shards(): cache = lax.all_gather(cache_kv, 'page', axis=1, tiled=True)]
    and x18 -> x0, other arithmetic: 10.9 us -> none  [the longest x16 9.78 us: one_step(): ((node_block[None, :] == leaf_node[:, None]) | (node_block[None, :] == up...]
    slice x2 -> x1, local copies, waits for them, and re-layouts: 6.86 us -> 0.09 us  [shards(): first_seg = segment[::Q_BLOCK]]
  transfers between devices with their start and end apart: 3 -> 3, of which waited for: 3 -> 3; matrix products, arithmetic and copies ran while one was open for 9% -> 3% of each run, Pallas kernels for 0% -> 0%
where the time goes in v1:
time: 237 us; the launch traced here: 235 us
  waiting for transfers between devices  117 us (49%)
  Pallas kernels  92.4 us (39%)
  between operations  13.2 us (6%)
  matrix products  5.95 us (3%)
  other arithmetic  4.18 us (2%)
    pallas_call x1, Pallas kernels, attention(): pl.pallas_call(attn_kernel, grid_spec=grid_spec, interpret=INTERPRET, out...  92.4 us
    all_gather x1, waiting for transfers between devices, shards(): cache = lax.all_gather(cache_kv, 'page', axis=1, tiled=True)  51.6 us
    reduce_scatter x1, waiting for transfers between devices, shards(): lax.psum_scatter(jnp.dot(attn, w_out, preferred_element_type=jnp.float32)...  33.7 us
    all_gather x1, waiting for transfers between devices, shards(): lax.all_gather(normed, 'head', axis=0, tiled=True)  30.5 us
  transfers between devices with their start and end apart: 3, of which 3 were waited for; matrix products, arithmetic and copies ran while one was open for 3% of the time, Pallas kernels for 0%

profile of v1, /device:TPU:1, one launch (start us, length us, event | category | flops | bytes accessed | tf_op | source)
XLA Modules:
  0.0 234.5 jit_solution(3054774582480579014)
XLA Ops:
  6.5 0.0 copy-start.4
  6.6 0.0 all-gather.3.cloned.1.call-start
  6.6 1.4 fusion
  8.0 2.0 fusion.2
  10.0 0.0 all-gather.3.cloned.1.call-update
  10.0 0.0 all-gather.5.cloned.1.call-start
  10.1 0.7 all-gather.5.cloned.1.call-update
  10.8 0.0 reduce-scatter.2.cloned.1.call-start
  10.8 0.1 slice.3
  10.9 0.1 select_reduce_fusion.2
  11.0 0.1 select_reduce_fusion.1
  11.1 0.1 select_reduce_fusion
  11.2 0.2 copy.19.tok_ref
  11.5 0.3 or_reduce_fusion
  11.8 0.1 reshape.55.vis_ref
  11.9 1.7 copy.18
  13.6 0.2 convert_reduce_fusion
  13.8 30.5 %all-gather.3.cloned.1.call-done = bf16[1024,1024]{1,0:T(8,128)(2,1)} async-done(((bf16[256,1024]{1,0:T(8,128)(2,1)}), bf16[1024,1024]{1,0:T(8,128)(2,1)}) %all-gather.3.cloned.1.call-update) | async-done | bytes 2097168 | tf_op jit(solution)/shard_map/all_gather | solution.py:165
  44.3 3.9 %convolution_convert_fusion.1.q_ref.kn_ref.vn_ref = bf16[1024,768]{1,0:T(8,128)(2,1)S(1)} fusion(bf16[1024,1024]{1,0:T(8,128)(2,1)} %all-gather.3.cloned.1.call-done, bf16[1024,768]{0,1:T(8,128)(2,1)} %bitcast.25), kind=kOutput, calls=%fused_computation.1 | convolution fusion | flops 1611399168 | bytes 5242880 | tf_op jit(solution)/shard_map/dot_general | solution.py:164
  48.1 51.6 %all-gather.5.cloned.1.call-done.cache_ref = bf16[2,64,128,256]{3,2,1,0:T(8,128)(2,1)} async-done(((bf16[2,2,128,256]{3,2,1,0:T(8,128)(2,1)}), bf16[2,64,128,256]{3,2,1,0:T(8,128)(2,1)}) %all-gather.5.cloned.1.call-update) | async-done | bytes 8388624 | tf_op jit(solution)/shard_map/all_gather | solution.py:189
  99.7 92.4 %shard_map.100 = bf16[1024,256]{1,0:T(8,128)(2,1)S(1)} custom-call(s32[512]{0:T(512)S(1)} %reshape.55.vis_ref, s32[64]{0:T(128)S(1)} %copy-done.2, s32[64]{0:T(128)S(1)} %copy-done.3, s32[8]{0:T(128)S(1)} %and_select_fusion.kfirst_ref, bf16[1024,768]{1,0:T(8,128)(2,1)S(1)} %convolution_convert_fusion.1.q_ref.kn_ref.vn_ref, s32[1024,4]{1,0:T(8,128)S(1)} %copy.19.tok_ref, ...), custom_call_target="tpu_custom_call" | custom-call | tf_op jit(solution)/shard_map/pallas_call | solution.py:132
  192.2 2.1 convolution_convert_fusion
  194.2 0.0 reduce-scatter.2.cloned.1.call-update
  194.3 33.7 %reduce-scatter.2.cloned.1.call-done = bf16[256,1024]{1,0:T(8,128)(2,1)} async-done(((bf16[1024,1024]{1,0:T(8,128)(2,1)}), bf16[256,1024]{1,0:T(8,128)(2,1)}) %reduce-scatter.2.cloned.1.call-update) | async-done | bytes 524304 | tf_op jit(solution)/shard_map/reduce_scatter | solution.py:191
  (17 shorter events, 0.1 us)
Async XLA Ops:
  6.5 185.6 %copy-start = (bf16[256,1024]{1,0:T(8,128)(2,1)S(1)}, bf16[256,1024]{1,0:T(8,128)(2,1)}, u32[]{:S(2)}) copy-start(bf16[256,1024]{1,0:T(8,128)(2,1)} %param.13) | copy-start | bytes 1572868
  6.5 4.3 %copy-start.1 = (s32[1,1024]{1,0:T(1,128)S(1)}, s32[1,1024]{1,0:T(1,128)}, u32[]{:S(2)}) copy-start(s32[1,1024]{1,0:T(1,128)} %param.18) | copy-start | bytes 12292
  6.5 4.4 %copy-start.6 = (s32[1,8]{1,0:T(1,128)S(1)}, s32[1,8]{1,0:T(1,128)}, u32[]{:S(2)}) copy-start(s32[1,8]{1,0:T(1,128)} %param.19) | copy-start | bytes 100
  6.5 4.5 %copy-start.5 = (s32[19]{0:T(128)S(1)}, s32[19]{0:T(128)}, u32[]{:S(2)}) copy-start(s32[19]{0:T(128)} %param.17) | copy-start | bytes 232
  6.5 4.9 %copy-start.2 = (s32[64]{0:T(128)S(1)}, s32[64]{0:T(128)}, u32[]{:S(2)}) copy-start(s32[64]{0:T(128)} %pnode_ref.1) | copy-start | bytes 772
  6.5 5.3 %copy-start.4 = (bf16[1024,3,256]{2,0,1:T(8,128)(2,1)S(1)}, bf16[1024,3,256]{2,0,1:T(8,128)(2,1)}, u32[]{:S(2)}) copy-start(bf16[1024,3,256]{2,0,1:T(8,128)(2,1)} %param.12) | copy-start | bytes 4718596
  6.6 37.7 %all-gather.3.cloned.1.call-start = ((), (), s32[]{:S(2)}) async-start(), calls=%async_computation.1 | async-start | bytes 2621440 | tf_op jit(solution)/shard_map/all_gather | solution.py:165
  10.0 89.7 %all-gather.5.cloned.1.call-start = ((), (), s32[]{:S(2)}) async-start(), calls=%async_computation.2 | async-start | bytes 8650752 | tf_op jit(solution)/shard_map/all_gather | solution.py:189
  10.8 217.2 %reduce-scatter.2.cloned.1.call-start = ((), (), s32[]{:S(2)}) async-start(), calls=%async_computation.3 | async-start | bytes 2621440 | tf_op jit(solution)/shard_map/reduce_scatter | solution.py:191
  44.3 55.5 %copy-start.3 = (s32[64]{0:T(128)S(1)}, s32[64]{0:T(128)}, u32[]{:S(2)}) copy-start(s32[64]{0:T(128)} %pfill_ref.1) | copy-start | bytes 772
Sparse Core Ops, SparseCore 0:
  10.2 34.0 all-gather.2
  46.6 53.0 all-gather.4
  194.4 33.5 reduce-scatter.1

commit v2 on v1

v2 whole, which is shorter than its diff:
```python
import jax
import jax.numpy as jnp
from jax import lax
from jax.experimental import pallas as pl
from jax.experimental.pallas import tpu as pltpu
from jax.sharding import PartitionSpec as P

HD = 64
EPSILON = 1e-06
FLOOR_SCORE = -1e30
Q_BLOCK = 128
K_BLOCK = 128
INTERPRET = False


def lookup(indices, lookup_table):
    matches = indices[:, None] == jnp.arange(lookup_table.shape[0], dtype=jnp.int32)[None, :]
    return jnp.sum(jnp.where(matches, lookup_table[None, :], 0), axis=1)


def attn_kernel(
    vis_ref, pnode_ref, pfill_ref, kfirst_ref,
    qt_ref, tok_ref, kn_ref, vnt_ref, segk_ref, ck_ref, cvt_ref,
    o_ref,
    m_sc, l_sc, acc_sc,
):
    i = pl.program_id(0)
    width, tq = qt_ref.shape
    groups = width // HD
    pages = ck_ref.shape[0]
    kb = ck_ref.shape[1]
    qt = qt_ref[...] * jnp.asarray(0.125, jnp.bfloat16)
    seg_q = tok_ref[0:1, :]
    leaf = tok_ref[1:2, :]
    upper = tok_ref[2:3, :]
    root = tok_ref[3:4, :]
    m_sc[...] = jnp.full(m_sc.shape, FLOOR_SCORE, jnp.float32)
    l_sc[...] = jnp.zeros(l_sc.shape, jnp.float32)
    acc_sc[...] = jnp.zeros(acc_sc.shape, jnp.float32)
    col_head = lax.broadcasted_iota(jnp.int32, (kb, width), 1) // HD
    row_head = lax.broadcasted_iota(jnp.int32, (width, kb), 0) // HD
    slot = lax.broadcasted_iota(jnp.int32, (kb, 1), 0)

    def update(k, vt, mask):
        zk = jnp.zeros_like(k)
        kbd = jnp.concatenate([jnp.where(col_head == h, k, zk) for h in range(groups)], axis=0)
        st = jnp.dot(kbd, qt, preferred_element_type=jnp.float32)
        probs = []
        scales = []
        for h in range(groups):
            s_h = jnp.where(mask, st[h * kb:(h + 1) * kb, :], FLOOR_SCORE)
            m_old = m_sc[h]
            m_new = jnp.maximum(m_old, jnp.max(s_h, axis=0, keepdims=True))
            alpha = jnp.exp(m_old - m_new)
            p_h = jnp.exp(s_h - m_new)
            l_sc[h] = alpha * l_sc[h] + jnp.sum(p_h, axis=0, keepdims=True)
            m_sc[h] = m_new
            probs.append(p_h.astype(jnp.bfloat16))
            scales.append(jnp.broadcast_to(alpha, (HD, tq)))
        zv = jnp.zeros_like(vt)
        vbdt = jnp.concatenate([jnp.where(row_head == h, vt, zv) for h in range(groups)], axis=1)
        pv = jnp.dot(vbdt, jnp.concatenate(probs, axis=0), preferred_element_type=jnp.float32)
        acc_sc[...] = acc_sc[...] * jnp.concatenate(scales, axis=0) + pv

    qpos = i * tq + lax.broadcasted_iota(jnp.int32, (1, tq), 1)

    def suffix_step(b, carry):
        start = pl.multiple_of(b * kb, kb)
        kpos = start + slot
        mask = (segk_ref[pl.ds(start, kb), :] == seg_q) & (kpos <= qpos)
        update(kn_ref[pl.ds(start, kb), :], vnt_ref[:, pl.ds(start, kb)], mask)
        return carry

    last = (i * tq + tq - 1) // kb
    lax.fori_loop(kfirst_ref[i], last + 1, suffix_step, 0)

    def page_step(g, carry):
        @pl.when(vis_ref[i * pages + g] > 0)
        def _():
            node = pnode_ref[g]
            fill = pfill_ref[g]
            tok_ok = (leaf == node) | (upper == node) | (root == node)
            mask = tok_ok & (slot < fill)
            update(ck_ref[g], cvt_ref[g], mask)

        return carry

    lax.fori_loop(0, pages, page_step, 0)

    norm = jnp.concatenate([jnp.broadcast_to(l_sc[h], (HD, tq)) for h in range(groups)], axis=0)
    o_ref[...] = (acc_sc[...] / norm).astype(o_ref.dtype)


def attention(vis, page_node, page_fill, kfirst, qt, tok, proj, vnt, segk, ck, cvt):
    width, tokens = qt.shape
    groups = width // HD
    nqb = tokens // Q_BLOCK
    grid_spec = pltpu.PrefetchScalarGridSpec(
        num_scalar_prefetch=4,
        grid=(nqb,),
        in_specs=[
            pl.BlockSpec((width, Q_BLOCK), lambda i, *_: (0, i)),
            pl.BlockSpec((tok.shape[0], Q_BLOCK), lambda i, *_: (0, i)),
            pl.BlockSpec((tokens, width), lambda i, *_: (0, 1)),
            pl.BlockSpec(memory_space=pltpu.VMEM),
            pl.BlockSpec(memory_space=pltpu.VMEM),
            pl.BlockSpec(memory_space=pltpu.VMEM),
            pl.BlockSpec(memory_space=pltpu.VMEM),
        ],
        out_specs=pl.BlockSpec((width, Q_BLOCK), lambda i, *_: (0, i)),
        scratch_shapes=[
            pltpu.VMEM((groups, 1, Q_BLOCK), jnp.float32),
            pltpu.VMEM((groups, 1, Q_BLOCK), jnp.float32),
            pltpu.VMEM((width, Q_BLOCK), jnp.float32),
        ],
    )
    return pl.pallas_call(
        attn_kernel,
        grid_spec=grid_spec,
        interpret=INTERPRET,
        out_shape=jax.ShapeDtypeStruct((width, tokens), jnp.bfloat16),
        compiler_params=pltpu.CompilerParams(
            dimension_semantics=("arbitrary",), vmem_limit_bytes=48 * 1024 * 1024
        ),
    )(vis, page_node, page_fill, kfirst, qt, tok, proj, vnt, segk, ck, cvt)


def shards(
    hidden_in,
    norm_gain,
    w_qkv,
    w_out,
    cache_kv,
    page_node,
    page_fill,
    node_parent,
    tok_seg,
    req_leaf,
):
    widened = hidden_in[0].astype(jnp.float32)
    normed = (
        widened
        * lax.rsqrt(jnp.mean(widened * widened, axis=1, keepdims=True) + EPSILON)
        * norm_gain
    ).astype(jnp.bfloat16)
    model_width = widened.shape[1]
    group_width = w_qkv.shape[2]
    weight_flat = w_qkv.reshape(model_width, 3 * group_width)
    projected = jnp.dot(
        lax.all_gather(normed, "head", axis=0, tiled=True),
        weight_flat,
        preferred_element_type=jnp.float32,
    ).astype(jnp.bfloat16)
    tokens = projected.shape[0]
    segment = tok_seg[0]
    leaf_node = lookup(segment, req_leaf[0])
    upper_node = lookup(leaf_node, node_parent)
    root_node = lookup(upper_node, node_parent)
    zero_row = jnp.zeros_like(segment)
    tok = jnp.stack(
        [segment, leaf_node, upper_node, root_node] + [zero_row] * 4, axis=0
    )
    pages = page_node.shape[0]
    seen = (
        (page_node[None, :] == leaf_node[:, None])
        | (page_node[None, :] == upper_node[:, None])
        | (page_node[None, :] == root_node[:, None])
    )
    nqb = tokens // Q_BLOCK
    vis = jnp.any(seen.reshape(nqb, Q_BLOCK, pages), axis=1).astype(jnp.int32).reshape(-1)
    first_seg = segment[::Q_BLOCK]
    kfirst = (
        jnp.sum((segment[None, :] < first_seg[:, None]).astype(jnp.int32), axis=1) // K_BLOCK
    ).astype(jnp.int32)
    segk = segment[:, None]
    qt = projected[:, :group_width].T
    vnt = projected[:, 2 * group_width:].T
    ck = lax.all_gather(cache_kv[0], "page", axis=0, tiled=True)
    cvt = lax.all_gather(jnp.swapaxes(cache_kv[1], 1, 2), "page", axis=0, tiled=True)
    attn_t = attention(vis, page_node, page_fill, kfirst, qt, tok, projected, vnt, segk, ck, cvt)
    result = lax.psum_scatter(
        lax.dot_general(
            attn_t, w_out, (((0,), (0,)), ((), ())), preferred_element_type=jnp.float32
        ).astype(jnp.bfloat16),
        "head",
        scatter_dimension=0,
        tiled=True,
    )
    return result[None]


def solution(mesh):
    placed = (
        P("page", "head", None),
        P(),
        P(None, None, "head"),
        P("head", None),
        P(None, "page", None, "head"),
        P(),
        P(),
        P(),
        P("page", None),
        P("page", None),
    )
    return jax.shard_map(
        shards, mesh=mesh, in_specs=placed, out_specs=P("page", "head", None), check_vma=False
    )
```

time: 237 us -> 264 us (1.11); the launches traced: 235 us -> 265 us
  waiting for transfers between devices: 117 us -> 152 us
  Pallas kernels: 92.4 us -> 79.6 us
  local copies, waits for them, and re-layouts: 2.14 us -> 8.48 us
    all_gather x1 -> x2, waiting for transfers between devices: 51.6 us -> 87.3 us  [the longest x1 47.6 us: shards(): ck = lax.all_gather(cache_kv[0], 'page', axis=0, tiled=True)]
    pallas_call x1, Pallas kernels: 92.4 us -> 79.6 us  [attention(): pl.pallas_call(attn_kernel, grid_spec=grid_spec, interpret=INTERPRET, out...]
  transfers between devices with their start and end apart: 3 -> 4, of which waited for: 3 -> 4; matrix products, arithmetic and copies ran while one was open for 3% -> 5% of each run, Pallas kernels for 0% -> 0%
where the time goes in v2:
time: 264 us; the launch traced here: 265 us
  waiting for transfers between devices  152 us (58%)
  Pallas kernels  79.6 us (30%)
  between operations  13.3 us (5%)
  local copies, waits for them, and re-layouts  8.48 us (3%)
  matrix products  7.19 us (3%)
  other arithmetic  4.17 us (2%)
    pallas_call x1, Pallas kernels, attention(): pl.pallas_call(attn_kernel, grid_spec=grid_spec, interpret=INTERPRET, out...  79.6 us
    all_gather x1, waiting for transfers between devices, shards(): ck = lax.all_gather(cache_kv[0], 'page', axis=0, tiled=True)  47.6 us
    all_gather x1, waiting for transfers between devices, shards(): lax.all_gather(jnp.swapaxes(cache_kv[1], 1, 2), 'page', axis=0, tiled=True)  39.7 us
    reduce_scatter x1, waiting for transfers between devices, shards(): lax.psum_scatter(lax.dot_general(attn_t, w_out, (((0,), (0,)), ((), ())),...  34.7 us
    all_gather x1, waiting for transfers between devices, shards(): lax.all_gather(normed, 'head', axis=0, tiled=True)  28.9 us
  transfers between devices with their start and end apart: 4, of which 4 were waited for; matrix products, arithmetic and copies ran while one was open for 5% of the time, Pallas kernels for 0%

profile of v2, /device:TPU:1, one launch (start us, length us, event | category | flops | bytes accessed | tf_op | source)
XLA Modules:
  0.0 264.5 jit_solution(17948778341242750290)
XLA Ops:
  6.6 1.4 fusion
  8.0 2.0 fusion.2
  10.1 0.7 fusion.3
  10.8 0.8 copy.33
  11.6 0.7 all-gather.9.cloned.1.call-update
  12.4 0.1 slice.15
  12.5 0.1 select_reduce_fusion.2
  12.6 0.1 select_reduce_fusion.1
  12.7 0.1 select_reduce_fusion
  12.8 0.3 or_reduce_fusion
  13.1 0.1 reshape.55.vis_ref
  13.1 1.7 copy.25
  14.9 0.2 copy.30.segk_ref
  15.2 0.2 convert_reduce_fusion
  15.4 28.9 %all-gather.5.cloned.1.call-done = bf16[1024,1024]{1,0:T(8,128)(2,1)} async-done(((bf16[256,1024]{1,0:T(8,128)(2,1)}), bf16[1024,1024]{1,0:T(8,128)(2,1)}) %all-gather.5.cloned.1.call-update) | async-done | bytes 2097168 | tf_op jit(solution)/shard_map/all_gather | solution.py:150
  44.2 5.1 %convolution_convert_fusion.1 = bf16[1024,768]{0,1:T(8,128)(2,1)} fusion(bf16[1024,1024]{1,0:T(8,128)(2,1)} %all-gather.5.cloned.1.call-done, bf16[1024,768]{0,1:T(8,128)(2,1)} %bitcast.30), kind=kOutput, calls=%fused_computation.1 | convolution fusion | flops 1611399168 | bytes 5242880 | tf_op jit(solution)/shard_map/dot_general | solution.py:149
  49.3 1.7 copy.29.kn_ref
  51.1 2.1 slice_bitcast_fusion
  53.1 39.7 %all-gather.7.cloned.1.call-done.cvt_ref = bf16[64,256,128]{2,1,0:T(8,128)(2,1)} async-done(((bf16[2,256,128]{2,1,0:T(8,128)(2,1)}), bf16[64,256,128]{2,1,0:T(8,128)(2,1)}) %all-gather.7.cloned.1.call-update) | async-done | bytes 4194320 | tf_op jit(solution)/shard_map/all_gather | solution.py:179
  92.8 47.6 %all-gather.9.cloned.1.call-done = bf16[1,64,128,256]{3,2,0,1:T(8,128)(2,1)} async-done(((bf16[1,2,128,256]{3,2,0,1:T(8,128)(2,1)}), bf16[1,64,128,256]{3,2,0,1:T(8,128)(2,1)}) %all-gather.9.cloned.1.call-update) | async-done | bytes 4194320 | tf_op jit(solution)/shard_map/all_gather | solution.py:178
  140.5 1.0 copy-done.1
  141.5 79.6 %shard_map.100 = bf16[256,1024]{1,0:T(8,128)(2,1)S(1)} custom-call(s32[512]{0:T(512)S(1)} %reshape.55.vis_ref, s32[64]{0:T(128)S(1)} %copy-done.2, s32[64]{0:T(128)S(1)} %copy-done.3, s32[8]{0:T(128)S(1)} %and_select_fusion.kfirst_ref, bf16[256,1024]{1,0:T(8,128)(2,1)S(1)} %copy-done.1, s32[8,1024]{1,0:T(8,128)S(1)} %stack.19.tok_ref, ...), custom_call_target="tpu_custom_call" | custom-call | tf_op jit(solution)/shard_map/pallas_call | solution.py:117
  221.1 2.1 convolution_convert_fusion
  223.3 34.7 %reduce-scatter.2.cloned.1.call-done = bf16[256,1024]{1,0:T(8,128)(2,1)} async-done(((bf16[1024,1024]{1,0:T(8,128)(2,1)}), bf16[256,1024]{1,0:T(8,128)(2,1)}) %reduce-scatter.2.cloned.1.call-update) | async-done | bytes 524304 | tf_op jit(solution)/shard_map/reduce_scatter | solution.py:181
  (29 shorter events, 0.3 us)
Async XLA Ops:
  6.5 214.6 %copy-start = (bf16[256,1024]{1,0:T(8,128)(2,1)S(1)}, bf16[256,1024]{1,0:T(8,128)(2,1)}, u32[]{:S(2)}) copy-start(bf16[256,1024]{1,0:T(8,128)(2,1)} %param.13) | copy-start | bytes 1572868
  6.5 3.6 %copy-start.5 = (bf16[2,2,128,256]{3,2,1,0:T(8,128)(2,1)S(1)}, bf16[2,2,128,256]{3,2,1,0:T(8,128)(2,1)}, u32[]{:S(2)}) copy-start(bf16[2,2,128,256]{3,2,1,0:T(8,128)(2,1)} %param.14) | copy-start | bytes 786436
  6.5 5.8 %copy-start.6 = (s32[1,1024]{1,0:T(1,128)S(1)}, s32[1,1024]{1,0:T(1,128)}, u32[]{:S(2)}) copy-start(s32[1,1024]{1,0:T(1,128)} %param.18) | copy-start | bytes 12292
  6.5 5.9 %copy-start.8 = (s32[1,8]{1,0:T(1,128)S(1)}, s32[1,8]{1,0:T(1,128)}, u32[]{:S(2)}) copy-start(s32[1,8]{1,0:T(1,128)} %param.19) | copy-start | bytes 100
  6.5 6.0 %copy-start.7 = (s32[19]{0:T(128)S(1)}, s32[19]{0:T(128)}, u32[]{:S(2)}) copy-start(s32[19]{0:T(128)} %param.17) | copy-start | bytes 232
  6.5 6.2 %copy-start.2 = (s32[64]{0:T(128)S(1)}, s32[64]{0:T(128)}, u32[]{:S(2)}) copy-start(s32[64]{0:T(128)} %pnode_ref.1) | copy-start | bytes 772
  6.6 6.6 %copy-start.4 = (bf16[1024,3,256]{2,0,1:T(8,128)(2,1)S(1)}, bf16[1024,3,256]{2,0,1:T(8,128)(2,1)}, u32[]{:S(2)}) copy-start(bf16[1024,3,256]{2,0,1:T(8,128)(2,1)} %param.12) | copy-start | bytes 4718596
  6.6 37.7 %all-gather.5.cloned.1.call-start = ((), (), s32[]{:S(2)}) async-start(), calls=%async_computation.1 | async-start | bytes 2621440 | tf_op jit(solution)/shard_map/all_gather | solution.py:150
  10.1 82.8 %all-gather.7.cloned.1.call-start = ((), (), s32[]{:S(2)}) async-start(), calls=%async_computation.2 | async-start | bytes 4325376 | tf_op jit(solution)/shard_map/all_gather | solution.py:179
  11.6 128.9 %all-gather.9.cloned.1.call-start = ((), (), s32[]{:S(2)}) async-start(), calls=%async_computation.4 | async-start | bytes 4325376 | tf_op jit(solution)/shard_map/all_gather | solution.py:178
  12.3 245.7 %reduce-scatter.2.cloned.1.call-start = ((), (), s32[]{:S(2)}) async-start(), calls=%async_computation.3 | async-start | bytes 2621440 | tf_op jit(solution)/shard_map/reduce_scatter | solution.py:181
  49.3 91.1 %copy-start.3 = (s32[64]{0:T(128)S(1)}, s32[64]{0:T(128)}, u32[]{:S(2)}) copy-start(s32[64]{0:T(128)} %pfill_ref.1) | copy-start | bytes 772
  140.5 1.0 copy-start.1
Sparse Core Ops, SparseCore 0:
  10.2 34.0 all-gather.4
  46.5 46.3 all-gather.6
  95.1 45.3 all-gather.8
  223.4 34.5 reduce-scatter.1

commit v3 on v2

--- a/solution.py
+++ b/solution.py
@@ -20,15 +20,24 @@
 
 def attn_kernel(
     vis_ref, pnode_ref, pfill_ref, kfirst_ref,
-    qt_ref, tok_ref, kn_ref, vnt_ref, segk_ref, ck_ref, cvt_ref,
+    qt_ref, tok_ref, kn_ref, vnt_ref, segk_ref, cache_ref,
     o_ref,
-    m_sc, l_sc, acc_sc,
+    m_sc, l_sc, acc_sc, cvt_ref,
 ):
     i = pl.program_id(0)
     width, tq = qt_ref.shape
     groups = width // HD
-    pages = ck_ref.shape[0]
-    kb = ck_ref.shape[1]
+    pages = cache_ref.shape[1]
+    kb = cache_ref.shape[2]
+
+    @pl.when(i == 0)
+    def _():
+        def transpose_page(g, carry):
+            cvt_ref[g] = cache_ref[1, g].astype(jnp.float32).T.astype(cvt_ref.dtype)
+            return carry
+
+        lax.fori_loop(0, pages, transpose_page, 0)
+
     qt = qt_ref[...] * jnp.asarray(0.125, jnp.bfloat16)
     seg_q = tok_ref[0:1, :]
     leaf = tok_ref[1:2, :]
@@ -81,7 +90,7 @@
             fill = pfill_ref[g]
             tok_ok = (leaf == node) | (upper == node) | (root == node)
             mask = tok_ok & (slot < fill)
-            update(ck_ref[g], cvt_ref[g], mask)
+            update(cache_ref[0, g], cvt_ref[g], mask)
 
         return carry
 
@@ -91,7 +100,7 @@
     o_ref[...] = (acc_sc[...] / norm).astype(o_ref.dtype)
 
 
-def attention(vis, page_node, page_fill, kfirst, qt, tok, proj, vnt, segk, ck, cvt):
+def attention(vis, page_node, page_fill, kfirst, qt, tok, proj, vnt, segk, cache):
     width, tokens = qt.shape
     groups = width // HD
     nqb = tokens // Q_BLOCK
@@ -105,13 +114,13 @@
             pl.BlockSpec(memory_space=pltpu.VMEM),
             pl.BlockSpec(memory_space=pltpu.VMEM),
             pl.BlockSpec(memory_space=pltpu.VMEM),
-            pl.BlockSpec(memory_space=pltpu.VMEM),
         ],
         out_specs=pl.BlockSpec((width, Q_BLOCK), lambda i, *_: (0, i)),
         scratch_shapes=[
             pltpu.VMEM((groups, 1, Q_BLOCK), jnp.float32),
             pltpu.VMEM((groups, 1, Q_BLOCK), jnp.float32),
             pltpu.VMEM((width, Q_BLOCK), jnp.float32),
+            pltpu.VMEM((cache.shape[1], width, cache.shape[2]), jnp.bfloat16),
         ],
     )
     return pl.pallas_call(
@@ -122,7 +131,7 @@
         compiler_params=pltpu.CompilerParams(
             dimension_semantics=("arbitrary",), vmem_limit_bytes=48 * 1024 * 1024
         ),
-    )(vis, page_node, page_fill, kfirst, qt, tok, proj, vnt, segk, ck, cvt)
+    )(vis, page_node, page_fill, kfirst, qt, tok, proj, vnt, segk, cache)
 
 
 def shards(
@@ -175,9 +184,8 @@
     segk = segment[:, None]
     qt = projected[:, :group_width].T
     vnt = projected[:, 2 * group_width:].T
-    ck = lax.all_gather(cache_kv[0], "page", axis=0, tiled=True)
-    cvt = lax.all_gather(jnp.swapaxes(cache_kv[1], 1, 2), "page", axis=0, tiled=True)
-    attn_t = attention(vis, page_node, page_fill, kfirst, qt, tok, projected, vnt, segk, ck, cvt)
+    cache = lax.all_gather(cache_kv, "page", axis=1, tiled=True)
+    attn_t = attention(vis, page_node, page_fill, kfirst, qt, tok, projected, vnt, segk, cache)
     result = lax.psum_scatter(
         lax.dot_general(
             attn_t, w_out, (((0,), (0,)), ((), ())), preferred_element_type=jnp.float32

time: 264 us -> 234 us (0.89); the launches traced: 265 us -> 238 us
  waiting for transfers between devices: 152 us -> 118 us
  Pallas kernels: 79.6 us -> 88.3 us
    all_gather x2 -> x1, waiting for transfers between devices: 87.3 us -> 46.6 us  [shards(): cache = lax.all_gather(cache_kv, 'page', axis=1, tiled=True)]
    pallas_call x1, Pallas kernels: 79.6 us -> 88.3 us  [attention(): pl.pallas_call(attn_kernel, grid_spec=grid_spec, interpret=INTERPRET, out...]
    reduce_scatter x1, waiting for transfers between devices: 34.7 us -> 40.3 us  [shards(): lax.psum_scatter(lax.dot_general(attn_t, w_out, (((0,), (0,)), ((), ())),...]
  transfers between devices with their start and end apart: 4 -> 3, of which waited for: 4 -> 3; matrix products, arithmetic and copies ran while one was open for 5% -> 5% of each run, Pallas kernels for 0% -> 0%
where the time goes in v3:
time: 234 us; the launch traced here: 238 us
  waiting for transfers between devices  118 us (50%)
  Pallas kernels  88.3 us (38%)
  between operations  13.2 us (6%)
  matrix products  7.21 us (3%)
  local copies, waits for them, and re-layouts  7.02 us (3%)
  other arithmetic  4.16 us (2%)
    pallas_call x1, Pallas kernels, attention(): pl.pallas_call(attn_kernel, grid_spec=grid_spec, interpret=INTERPRET, out...  88.3 us
    all_gather x1, waiting for transfers between devices, shards(): cache = lax.all_gather(cache_kv, 'page', axis=1, tiled=True)  46.6 us
    reduce_scatter x1, waiting for transfers between devices, shards(): lax.psum_scatter(lax.dot_general(attn_t, w_out, (((0,), (0,)), ((), ())),...  40.3 us
    all_gather x1, waiting for transfers between devices, shards(): lax.all_gather(normed, 'head', axis=0, tiled=True)  30.4 us
    dot_general x1, matrix products, shards(): jnp.dot(lax.all_gather(normed, 'head', axis=0, tiled=True), weight_flat,...  5.09 us
  transfers between devices with their start and end apart: 3, of which 3 were waited for; matrix products, arithmetic and copies ran while one was open for 5% of the time, Pallas kernels for 0%

profile of v3, /device:TPU:1, one launch (start us, length us, event | category | flops | bytes accessed | tf_op | source)
XLA Modules:
  0.0 238.0 jit_solution(17281710016890500929)
XLA Ops:
  6.6 0.0 all-gather.3.cloned.1.call-start
  6.6 1.4 fusion
  8.0 2.0 fusion.2
  10.0 0.0 all-gather.5.cloned.1.call-start
  10.1 0.7 all-gather.5.cloned.1.call-update
  10.8 0.0 reduce-scatter.2.cloned.1.call-start
  10.8 0.1 slice.9
  10.9 0.1 select_reduce_fusion.2
  11.0 0.1 select_reduce_fusion.1
  11.1 0.1 select_reduce_fusion
  11.2 0.3 or_reduce_fusion
  11.5 0.1 reshape.55.vis_ref
  11.6 1.7 copy.17
  13.3 0.2 copy.20.segk_ref
  13.6 0.2 convert_reduce_fusion
  13.8 30.4 %all-gather.3.cloned.1.call-done = bf16[1024,1024]{1,0:T(8,128)(2,1)} async-done(((bf16[256,1024]{1,0:T(8,128)(2,1)}), bf16[1024,1024]{1,0:T(8,128)(2,1)}) %all-gather.3.cloned.1.call-update) | async-done | bytes 2097168 | tf_op jit(solution)/shard_map/all_gather | solution.py:159
  44.3 5.1 %convolution_convert_fusion.1 = bf16[1024,768]{0,1:T(8,128)(2,1)} fusion(bf16[1024,1024]{1,0:T(8,128)(2,1)} %all-gather.3.cloned.1.call-done, bf16[1024,768]{0,1:T(8,128)(2,1)} %bitcast.23), kind=kOutput, calls=%fused_computation.1 | convolution fusion | flops 1611399168 | bytes 5242880 | tf_op jit(solution)/shard_map/dot_general | solution.py:158
  49.4 1.7 copy.19.kn_ref
  51.1 2.1 slice_bitcast_fusion
  53.1 46.6 %all-gather.5.cloned.1.call-done.cache_ref = bf16[2,64,128,256]{3,2,1,0:T(8,128)(2,1)} async-done(((bf16[2,2,128,256]{3,2,1,0:T(8,128)(2,1)}), bf16[2,64,128,256]{3,2,1,0:T(8,128)(2,1)}) %all-gather.5.cloned.1.call-update) | async-done | bytes 8388624 | tf_op jit(solution)/shard_map/all_gather | solution.py:187
  99.7 1.0 copy-done.1
  100.8 88.3 %shard_map.100 = bf16[256,1024]{1,0:T(8,128)(2,1)S(1)} custom-call(s32[512]{0:T(512)S(1)} %reshape.55.vis_ref, s32[64]{0:T(128)S(1)} %copy-done.2, s32[64]{0:T(128)S(1)} %copy-done.3, s32[8]{0:T(128)S(1)} %and_select_fusion.kfirst_ref, bf16[256,1024]{1,0:T(8,128)(2,1)S(1)} %copy-done.1, s32[8,1024]{1,0:T(8,128)S(1)} %stack.19.tok_ref, ...), custom_call_target="tpu_custom_call" | custom-call | tf_op jit(solution)/shard_map/pallas_call | solution.py:126
  189.1 2.1 convolution_convert_fusion
  191.2 40.3 %reduce-scatter.2.cloned.1.call-done = bf16[256,1024]{1,0:T(8,128)(2,1)} async-done(((bf16[1024,1024]{1,0:T(8,128)(2,1)}), bf16[256,1024]{1,0:T(8,128)(2,1)}) %reduce-scatter.2.cloned.1.call-update) | async-done | bytes 524304 | tf_op jit(solution)/shard_map/reduce_scatter | solution.py:189
  (22 shorter events, 0.1 us)
Async XLA Ops:
  6.5 182.6 %copy-start = (bf16[256,1024]{1,0:T(8,128)(2,1)S(1)}, bf16[256,1024]{1,0:T(8,128)(2,1)}, u32[]{:S(2)}) copy-start(bf16[256,1024]{1,0:T(8,128)(2,1)} %param.13) | copy-start | bytes 1572868
  6.5 4.3 %copy-start.5 = (s32[1,1024]{1,0:T(1,128)S(1)}, s32[1,1024]{1,0:T(1,128)}, u32[]{:S(2)}) copy-start(s32[1,1024]{1,0:T(1,128)} %param.18) | copy-start | bytes 12292
  6.5 4.4 %copy-start.7 = (s32[1,8]{1,0:T(1,128)S(1)}, s32[1,8]{1,0:T(1,128)}, u32[]{:S(2)}) copy-start(s32[1,8]{1,0:T(1,128)} %param.19) | copy-start | bytes 100
  6.5 4.5 %copy-start.6 = (s32[19]{0:T(128)S(1)}, s32[19]{0:T(128)}, u32[]{:S(2)}) copy-start(s32[19]{0:T(128)} %param.17) | copy-start | bytes 232
  6.5 4.7 %copy-start.2 = (s32[64]{0:T(128)S(1)}, s32[64]{0:T(128)}, u32[]{:S(2)}) copy-start(s32[64]{0:T(128)} %pnode_ref.1) | copy-start | bytes 772
  6.5 5.1 %copy-start.4 = (bf16[1024,3,256]{2,0,1:T(8,128)(2,1)S(1)}, bf16[1024,3,256]{2,0,1:T(8,128)(2,1)}, u32[]{:S(2)}) copy-start(bf16[1024,3,256]{2,0,1:T(8,128)(2,1)} %param.12) | copy-start | bytes 4718596
  6.6 37.7 %all-gather.3.cloned.1.call-start = ((), (), s32[]{:S(2)}) async-start(), calls=%async_computation.1 | async-start | bytes 2621440 | tf_op jit(solution)/shard_map/all_gather | solution.py:159
  10.0 89.7 %all-gather.5.cloned.1.call-start = ((), (), s32[]{:S(2)}) async-start(), calls=%async_computation.2 | async-start | bytes 8650752 | tf_op jit(solution)/shard_map/all_gather | solution.py:187
  10.8 220.7 %reduce-scatter.2.cloned.1.call-start = ((), (), s32[]{:S(2)}) async-start(), calls=%async_computation.3 | async-start | bytes 2621440 | tf_op jit(solution)/shard_map/reduce_scatter | solution.py:189
  49.4 50.4 %copy-start.3 = (s32[64]{0:T(128)S(1)}, s32[64]{0:T(128)}, u32[]{:S(2)}) copy-start(s32[64]{0:T(128)} %pfill_ref.1) | copy-start | bytes 772
  99.7 1.0 copy-start.1
Sparse Core Ops, SparseCore 0:
  10.2 34.0 all-gather.2
  46.6 53.0 all-gather.4
  191.4 40.0 reduce-scatter.1
